TPU v7x, 32 devices: a whole 2x2x4 slice. The times are simulated.
32 devices in a mesh: dp: 8 (over y, x, core), tensor: 4 (over z).
Axes of the slice: x: 2, y: 2, z: 4, core: 2. Of those that a mesh axis runs over, the one named last changes fastest.
Arguments:
- teacher_master: float32 [256, 16384], P('dp', 'tensor'), as said below
- student_weight: bfloat16 [256, 16384], P('dp', 'tensor'), may hold values from -6 to 6
- teacher_feat: bfloat16 [2048, 256], P('dp'), as said below
- student_feat: bfloat16 [2048, 256], P('dp'), may hold values from -6 to 6
- center: float32 [16384], P('tensor'), may hold values from -0.3 to 0.3
Outputs:
- master_new: float32 [256, 16384], P('dp', 'tensor')
- student_grad: float32 [256, 16384], P('dp', 'tensor')
- new_center: float32 [16384], P('tensor')
Inputs may be any that keep to these rules, and one draw needn't show every extreme that they name: `teacher_feat`: rows of teacher features are real-valued and of order one. `teacher_master`: entries of the teacher master are real-valued and of order one.
All inputs are finite; a program needn't handle non-finite values.
Results may differ from a plain program's by a relative error of at most 0.014.
Values may be sent and summed in bfloat16 or wider, within the bound.
No kernel may reach another device: no remote copies, remote signals or barrier semaphores. Data moves between devices by JAX's collectives and lax.ppermute only.
A program may use at most 64 MiB of HBM per device.

v0:
```python
import jax
import jax.numpy as jnp
from jax import lax
from jax.sharding import PartitionSpec as P


def unit_rows(feat):
    wide = feat.astype(jnp.float32)
    return (wide * lax.rsqrt(jnp.sum(wide * wide, 1, keepdims=True) + 1e-06)).astype(jnp.bfloat16)


def shards(teacher_master, student_weight, teacher_feat, student_feat, center):
    zt = unit_rows(teacher_feat)
    zs = unit_rows(student_feat)
    images_all = teacher_feat.shape[0] * lax.axis_size("dp")
    student_full = lax.all_gather(student_weight, "dp", axis=0, tiled=True)
    master_new = 0.996 * teacher_master + 0.004 * student_weight.astype(jnp.float32)
    weight = lax.all_gather(master_new.astype(jnp.bfloat16), "dp", axis=0, tiled=True)
    feats = zt
    raw = jnp.dot(feats, weight, preferred_element_type=jnp.float32)
    squares = jnp.sum(jnp.square(weight.astype(jnp.float32)), 0)
    t_norm = jnp.sqrt(squares + 1e-06)
    t_cos = raw / t_norm
    s_norm = jnp.sqrt(jnp.sum(jnp.square(student_full.astype(jnp.float32)), 0) + 1e-06)
    s_cos = jnp.dot(zs, student_full, preferred_element_type=jnp.float32) / s_norm
    t_exp = jnp.exp((t_cos - center) / 0.04)
    s_exp = jnp.exp(s_cos / 0.1)
    t_total, s_total = lax.psum(
        (jnp.sum(t_exp, 1, keepdims=True), jnp.sum(s_exp, 1, keepdims=True)), "tensor"
    )
    cos_mean = lax.psum(jnp.sum(t_cos, 0), "dp") / images_all
    new_center = 0.5 * center + 0.5 * cos_mean
    dlog = ((s_exp / s_total - t_exp / t_total) / 0.1).astype(jnp.bfloat16)
    weighted = jnp.sum(dlog.astype(jnp.float32) * s_cos, 0)
    scaled = weighted / s_norm
    feats = zs
    product = lax.dot_general(
        feats, dlog, (((0,), (0,)), ((), ())), preferred_element_type=jnp.float32
    )
    student_grad = lax.psum_scatter(
        (product - student_full.astype(jnp.float32) * scaled) / s_norm,
        "dp",
        scatter_dimension=0,
        tiled=True,
    )
    return (master_new, student_grad, new_center)


def solution(mesh):
    placed = (P("dp", "tensor"), P("dp", "tensor"), P("dp", None), P("dp", None), P("tensor"))
    return jax.shard_map(
        shards,
        mesh=mesh,
        in_specs=placed,
        out_specs=(P("dp", "tensor"), P("dp", "tensor"), P("tensor")),
        check_vma=False,
    )
```

profile of v0, /device:TPU:0, one launch (start us, length us, event | category | flops | bytes accessed | tf_op | source)
XLA Modules:
  0.0 153.8 jit_solution(11268141412257356897)
XLA Ops:
  7.2 0.0 copy-start.3
  7.2 0.0 all-gather.3.cloned.1.call-start
  7.2 0.7 all-gather.3.cloned.1.call-update
  7.9 0.0 all-gather.5.cloned.1.call-start
  8.0 2.1 %fusion.13 = (bf16[32,4096]{1,0:T(8,128)(2,1)}, f32[32,4096]{1,0:T(8,128)}) fusion(bf16[32,4096]{1,0:T(8,128)(2,1)} %param.6, f32[32,4096]{1,0:T(8,128)} %param.5), kind=kLoop, calls=%fused_computation.31 | loop fusion | flops 655360 | bytes 1572864 | tf_op jit(solution)/shard_map/convert_element_type | solution.py:18
  10.0 0.0 all-gather.5.cloned.1.call-update
  10.1 0.0 reduce-scatter.2.cloned.1.call-start
  10.1 1.0 fusion.6
  11.1 1.0 fusion.4
  12.2 28.3 %all-gather.3.cloned.1.call-done = bf16[256,4096]{1,0:T(8,128)(2,1)} async-done(((bf16[32,4096]{1,0:T(8,128)(2,1)}), bf16[256,4096]{1,0:T(8,128)(2,1)}) %all-gather.3.cloned.1.call-update) | async-done | bytes 2097168 | tf_op jit(solution)/shard_map/all_gather | solution.py:16
  40.5 0.0 copy-start
  40.5 2.2 %fusion.1 = f32[4096]{0:T(1024)S(1)} fusion(bf16[256,4096]{1,0:T(8,128)(2,1)} %all-gather.3.cloned.1.call-done), kind=kLoop, calls=%fused_computation.6 | loop fusion | flops 3141632 | bytes 2113536 | tf_op jit(solution)/shard_map/reduce_sum | solution.py:24
  42.7 28.2 %all-gather.5.cloned.1.call-done = bf16[256,4096]{1,0:T(8,128)(2,1)} async-done(((bf16[32,4096]{1,0:T(8,128)(2,1)}), bf16[256,4096]{1,0:T(8,128)(2,1)}) %all-gather.5.cloned.1.call-update) | async-done | bytes 2097168 | tf_op jit(solution)/shard_map/all_gather | solution.py:18
  70.9 2.0 %multiply_reduce_fusion.1 = f32[4096]{0:T(1024)S(1)} fusion(bf16[256,4096]{1,0:T(8,128)(2,1)} %all-gather.5.cloned.1.call-done), kind=kLoop, calls=%fused_computation.10 | loop fusion | flops 3141632 | bytes 2113536 | tf_op jit(solution)/shard_map/reduce_sum | solution.py:21
  73.0 0.0 copy-done.3
  73.0 0.0 copy-done
  73.0 0.0 copy-start.1
  73.0 0.0 copy-start.2
  73.0 0.0 copy-start.4
  73.0 3.1 %fusion.2 = (f32[256]{0:T(256)S(1)}, f32[256,4096]{1,0:T(8,128)}) fusion(f32[4096]{0:T(1024)S(1)} %add_sqrt_fusion.1, bf16[256,4096]{1,0:T(8,128)(2,1)S(1)} %copy-done, bf16[256,256]{1,0:T(8,128)(2,1)S(1)} %copy-done.3, f32[256]{0:T(256)S(1)} %add_rsqrt_fusion.1), kind=kOutput, calls=%fused_computation.12 | convolution fusion | flops 540212992 | bytes 6440960 | tf_op jit(solution)/shard_map/dot_general | solution.py:25
  76.1 0.0 copy-done.1
  76.1 0.0 copy-done.2
  76.1 0.0 copy-done.4
  76.1 3.4 %fusion.12 = (f32[4096]{0:T(1024)S(1)}, f32[256]{0:T(256)S(1)}, f32[256,4096]{1,0:T(8,128)}) fusion(f32[4096]{0:T(1024)S(1)} %copy-done.4, f32[4096]{0:T(1024)S(1)} %add_sqrt_fusion, bf16[256,4096]{1,0:T(8,128)(2,1)S(1)} %copy-done.1, bf16[256,256]{1,0:T(8,128)(2,1)S(1)} %copy-done.2, f32[256]{0:T(256)S(1)} %add_rsqrt_fusion), kind=kOutput, calls=%fused_computation.30 | convolution fusion | flops 542306048 | bytes 6473728 | tf_op jit(solution)/shard_map/dot_general | solution.py:20
  79.5 11.7 %all-reduce = (f32[256]{0:T(256)S(1)}, f32[256]{0:T(256)S(1)}) all-reduce(f32[256]{0:T(256)S(1)} %get-tuple-element.4, f32[256]{0:T(256)S(1)} %get-tuple-element.12), channel_id=1, replica_groups=mesh['dp'=8,'tensor'=4] {'tensor'}, use_global_device_ids=true, to_apply=%region_7.0 | all-reduce | flops 512 | bytes 4096 | tf_op jit(solution)/shard_map/psum | solution.py:28
  91.1 4.5 %multiply_reduce_fusion = (f32[4096]{0:T(1024)S(1)}, bf16[256,4096]{1,0:T(8,128)(2,1)S(1)}) fusion(f32[256,4096]{1,0:T(8,128)} %get-tuple-element.13, f32[256]{0:T(256)S(1)} %get-tuple-element.5, f32[256,4096]{1,0:T(8,128)} %get-tuple-element.11, f32[4096]{0:T(1024)S(1)} %copy-done.4, f32[256]{0:T(256)S(1)} %get-tuple-element.6), kind=kLoop, calls=%fused_computation.7 | loop fusion | flops 11530240 | bytes 10520576 | tf_op jit(solution)/shard_map/reduce_sum | solution.py:34
  95.6 3.0 %fusion = f32[256,4096]{1,0:T(8,128)} fusion(bf16[256,4096]{1,0:T(8,128)(2,1)S(1)} %get-tuple-element.8, bf16[256,4096]{1,0:T(8,128)(2,1)S(1)} %copy-done, f32[4096]{0:T(1024)S(1)} %rsqrt_multiply_fusion, f32[4096]{0:T(1024)S(1)} %add_sqrt_fusion.1, bf16[256,256]{1,0:T(8,128)(2,1)S(1)} %copy-done.3, f32[256]{0:T(256)S(1)} %add_rsqrt_fusion.1), kind=kOutput, calls=%fused_computation.5 | convolution fusion | flops 541261824 | bytes 8553472 | tf_op jit(solution)/shard_map/dot_general | solution.py:37
  98.6 0.0 reduce-scatter.2.cloned.1.call-update
  98.6 22.4 %psum.23 = f32[4096]{0:T(1024)S(1)} all-reduce(f32[4096]{0:T(1024)S(1)} %get-tuple-element.3), channel_id=1, replica_groups=mesh['dp'=8,'tensor'=4] {'dp'}, use_global_device_ids=true, to_apply=%region_11.0 | all-reduce | flops 4096 | bytes 32768 | tf_op jit(solution)/shard_map/psum | solution.py:31
  121.0 0.6 multiply_add_fusion.1
  121.6 25.7 %reduce-scatter.2.cloned.1.call-done = f32[32,4096]{1,0:T(8,128)} async-done(((f32[256,4096]{1,0:T(8,128)}), f32[32,4096]{1,0:T(8,128)}) %reduce-scatter.2.cloned.1.call-update) | async-done | bytes 524304 | tf_op jit(solution)/shard_map/reduce_scatter | solution.py:40
  (5 shorter events, 0.0 us)
Async XLA Ops:
  7.2 65.8 %copy-start.3 = (bf16[256,256]{1,0:T(8,128)(2,1)S(1)}, bf16[256,256]{1,0:T(8,128)(2,1)}, u32[]{:S(2)}) copy-start(bf16[256,256]{1,0:T(8,128)(2,1)} %param.8) | copy-start | bytes 393220
  7.2 33.4 %all-gather.3.cloned.1.call-start = ((), (), s32[]{:S(2)}) async-start(), calls=%async_computation.1 | async-start | bytes 2359296 | tf_op jit(solution)/shard_map/all_gather | solution.py:16
  7.9 63.0 %all-gather.5.cloned.1.call-start = ((), (), s32[]{:S(2)}) async-start(), calls=%async_computation.2 | async-start | bytes 2359296 | tf_op jit(solution)/shard_map/all_gather | solution.py:18
  10.1 137.2 %reduce-scatter.2.cloned.1.call-start = ((), (), s32[]{:S(2)}) async-start(), calls=%async_computation.3 | async-start | bytes 4718592 | tf_op jit(solution)/shard_map/reduce_scatter | solution.py:40
  40.5 32.5 %copy-start = (bf16[256,4096]{1,0:T(8,128)(2,1)S(1)}, bf16[256,4096]{1,0:T(8,128)(2,1)}, u32[]{:S(2)}) copy-start(bf16[256,4096]{1,0:T(8,128)(2,1)} %all-gather.3.cloned.1.call-done) | copy-start | bytes 6291460
  73.0 3.1 %copy-start.1 = (bf16[256,4096]{1,0:T(8,128)(2,1)S(1)}, bf16[256,4096]{1,0:T(8,128)(2,1)}, u32[]{:S(2)}) copy-start(bf16[256,4096]{1,0:T(8,128)(2,1)} %all-gather.5.cloned.1.call-done) | copy-start | bytes 6291460
  73.0 3.1 %copy-start.2 = (bf16[256,256]{1,0:T(8,128)(2,1)S(1)}, bf16[256,256]{1,0:T(8,128)(2,1)}, u32[]{:S(2)}) copy-start(bf16[256,256]{1,0:T(8,128)(2,1)} %param.7) | copy-start | bytes 393220
  73.0 3.1 %copy-start.4 = (f32[4096]{0:T(1024)S(1)}, f32[4096]{0:T(1024)}, u32[]{:S(2)}) copy-start(f32[4096]{0:T(1024)} %param.9) | copy-start | bytes 49156
Sparse Core Ops, SparseCore 0:
  9.9 30.5 all-gather.2
  43.0 27.8 all-gather.4
  98.7 48.5 reduce-scatter.1
where the time goes:
time: 154 us
  waiting for transfers between devices  82.9 us (54%)
  blocking collectives  34.1 us (22%)
  between operations  13.9 us (9%)
  other arithmetic  13.4 us (9%)
  matrix products  9.39 us (6%)
    all_gather x1, waiting for transfers between devices, shards(): student_full = lax.all_gather(student_weight, 'dp', axis=0, tiled=True)  28.3 us
    all_gather x1, waiting for transfers between devices, shards(): lax.all_gather(master_new.astype(jnp.bfloat16), 'dp', axis=0, tiled=True)  28.2 us
    reduce_scatter x1, waiting for transfers between devices, shards(): lax.psum_scatter((product - student_full.astype(jnp.float32) * scaled) /...  25.7 us
    psum x1, blocking collectives, shards(): cos_mean = lax.psum(jnp.sum(t_cos, 0), 'dp') / images_all  22.4 us
    psum x1, blocking collectives, shards(): lax.psum((jnp.sum(t_exp, 1, keepdims=True), jnp.sum(s_exp, 1, keepdims=Tr...  11.7 us
    reduce_sum x1, other arithmetic, shards(): weighted = jnp.sum(dlog.astype(jnp.float32) * s_cos, 0)  4.47 us
    dot_general x1, matrix products, shards(): raw = jnp.dot(feats, weight, preferred_element_type=jnp.float32)  3.37 us
  transfers between devices with their start and end apart: 3, of which 3 were waited for; matrix products, arithmetic and copies ran while one was open for 5% of the time, Pallas kernels for 0%

commit v1 on v0

--- a/solution.py
+++ b/solution.py
@@ -13,7 +13,19 @@
     zt = unit_rows(teacher_feat)
     zs = unit_rows(student_feat)
     images_all = teacher_feat.shape[0] * lax.axis_size("dp")
-    student_full = lax.all_gather(student_weight, "dp", axis=0, tiled=True)
+    ready = jax.lax.axis_size("dp")
+    parts_out = jax.lax.axis_index("dp")
+    v_next, val, odd = (ready, parts_out, student_weight.shape[0])
+    heap = [(dd, (dd + 1) % v_next) for dd in range(v_next)]
+    student_full = jnp.zeros(
+        (*student_weight.shape[:0], v_next * odd, *student_weight.shape[1:]), student_weight.dtype
+    )
+    k_now = student_weight
+    for rr in range(v_next):
+        x_new = (val - rr) % v_next
+        student_full = lax.dynamic_update_slice_in_dim(student_full, k_now, x_new * odd, axis=0)
+        if rr < v_next - 1:
+            k_now = jax.lax.ppermute(k_now, perm=heap, axis_name="dp")
     master_new = 0.996 * teacher_master + 0.004 * student_weight.astype(jnp.float32)
     weight = lax.all_gather(master_new.astype(jnp.bfloat16), "dp", axis=0, tiled=True)
     feats = zt

time: 154 us -> 144 us (0.935)
  waiting for transfers between devices: 82.9 us -> 73.1 us
  other arithmetic: 13.4 us -> 10.8 us
  matrix products: 9.39 us -> 11 us
    ppermute x0 -> x7, waiting for transfers between devices: none -> 46.7 us  [shards(): k_now = jax.lax.ppermute(k_now, perm=heap, axis_name='dp')]
    all_gather x1 -> x0, waiting for transfers between devices: 28.3 us -> none  [shards(): student_full = lax.all_gather(student_weight, 'dp', axis=0, tiled=True)]
    all_gather x1, waiting for transfers between devices: 28.2 us -> 0.01 us  [shards(): lax.all_gather(master_new.astype(jnp.bfloat16), 'dp', axis=0, tiled=True)]
    reduce_sum x1, other arithmetic: 2.18 us -> 0.44 us  [shards(): jnp.sum(jnp.square(student_full.astype(jnp.float32)), 0) + 1e-06]
    dot_general x1, matrix products: 3.37 us -> 4.94 us  [shards(): raw = jnp.dot(feats, weight, preferred_element_type=jnp.float32)]
  transfers between devices with their start and end apart: 3 -> 9, of which waited for: 3 -> 8; matrix products, arithmetic and copies ran while one was open for 5% -> 5% of each run, Pallas kernels for 0% -> 0%
where the time goes in v1:
time: 144 us
  waiting for transfers between devices  73.1 us (51%)
  blocking collectives  34 us (24%)
  between operations  14.4 us (10%)
  matrix products  11 us (8%)
  other arithmetic  10.8 us (8%)
    ppermute x7, waiting for transfers between devices, shards(): k_now = jax.lax.ppermute(k_now, perm=heap, axis_name='dp')  46.7 us
    reduce_scatter x1, waiting for transfers between devices, shards(): lax.psum_scatter((product - student_full.astype(jnp.float32) * scaled) /...  26.3 us
    psum x1, blocking collectives, shards(): cos_mean = lax.psum(jnp.sum(t_cos, 0), 'dp') / images_all  22.3 us
    psum x1, blocking collectives, shards(): lax.psum((jnp.sum(t_exp, 1, keepdims=True), jnp.sum(s_exp, 1, keepdims=Tr...  11.7 us
    dot_general x1, matrix products, shards(): raw = jnp.dot(feats, weight, preferred_element_type=jnp.float32)  4.94 us
    reduce_sum x1, other arithmetic, shards(): weighted = jnp.sum(dlog.astype(jnp.float32) * s_cos, 0)  4.47 us
    dot_general x1, matrix products, shards(): jnp.dot(zs, student_full, preferred_element_type=jnp.float32) / s_norm  3.06 us
    dot_general x1, matrix products, shards(): lax.dot_general(feats, dlog, (((0,), (0,)), ((), ())), preferred_element_...  2.95 us
  transfers between devices with their start and end apart: 9, of which 8 were waited for; matrix products, arithmetic and copies ran while one was open for 5% of the time, Pallas kernels for 0%

profile of v1, /device:TPU:0, one launch (start us, length us, event | category | flops | bytes accessed | tf_op | source)
XLA Modules:
  0.0 144.2 jit_solution(6435399175421276920)
XLA Ops:
  7.2 0.0 copy-start
  7.2 0.0 copy-start.2
  7.2 0.0 all-gather.2.cloned.1.call-start
  7.2 0.5 collective-permute-start
  7.7 2.1 %fusion.17 = (bf16[32,4096]{1,0:T(8,128)(2,1)}, f32[32,4096]{1,0:T(8,128)}) fusion(bf16[32,4096]{1,0:T(8,128)(2,1)} %param.6, f32[32,4096]{1,0:T(8,128)} %param.5), kind=kLoop, calls=%fused_computation.40 | loop fusion | flops 655360 | bytes 1572864 | tf_op jit(solution)/shard_map/convert_element_type | solution.py:30
  9.8 0.0 all-gather.2.cloned.1.call-update
  9.8 0.0 reduce-scatter.2.cloned.1.call-start
  9.9 1.0 fusion.7
  10.9 0.2 broadcast_in_dim.6
  11.2 0.0 copy-done
  11.2 0.0 copy-done.2
  11.2 0.1 fusion.5
  11.5 3.4 %collective-permute-done = bf16[32,4096]{1,0:T(8,128)(2,1)S(1)} collective-permute-done((bf16[32,4096]{1,0:T(8,128)(2,1)}, bf16[32,4096]{1,0:T(8,128)(2,1)S(1)}, u32[]{:S(2)}, u32[]{:S(2)}) %collective-permute-start) | collective-permute-done | bytes 262176 | tf_op jit(solution)/shard_map/ppermute | solution.py:28
  14.9 0.0 collective-permute-start.1
  14.9 6.7 %collective-permute-done.1 = bf16[32,4096]{1,0:T(8,128)(2,1)S(1)} collective-permute-done((bf16[32,4096]{1,0:T(8,128)(2,1)S(1)}, bf16[32,4096]{1,0:T(8,128)(2,1)S(1)}, u32[]{:S(2)}, u32[]{:S(2)}) %collective-permute-start.1) | collective-permute-done | bytes 262176 | tf_op jit(solution)/shard_map/ppermute | solution.py:28
  21.6 0.0 collective-permute-start.2
  21.6 8.2 %collective-permute-done.2 = bf16[32,4096]{1,0:T(8,128)(2,1)S(1)} collective-permute-done((bf16[32,4096]{1,0:T(8,128)(2,1)S(1)}, bf16[32,4096]{1,0:T(8,128)(2,1)S(1)}, u32[]{:S(2)}, u32[]{:S(2)}) %collective-permute-start.2) | collective-permute-done | bytes 262176 | tf_op jit(solution)/shard_map/ppermute | solution.py:28
  29.8 0.0 collective-permute-start.3
  29.8 8.5 %collective-permute-done.3 = bf16[32,4096]{1,0:T(8,128)(2,1)S(1)} collective-permute-done((bf16[32,4096]{1,0:T(8,128)(2,1)S(1)}, bf16[32,4096]{1,0:T(8,128)(2,1)S(1)}, u32[]{:S(2)}, u32[]{:S(2)}) %collective-permute-start.3) | collective-permute-done | bytes 262176 | tf_op jit(solution)/shard_map/ppermute | solution.py:28
  38.3 0.0 collective-permute-start.4
  38.3 6.7 %collective-permute-done.4 = bf16[32,4096]{1,0:T(8,128)(2,1)S(1)} collective-permute-done((bf16[32,4096]{1,0:T(8,128)(2,1)S(1)}, bf16[32,4096]{1,0:T(8,128)(2,1)S(1)}, u32[]{:S(2)}, u32[]{:S(2)}) %collective-permute-start.4) | collective-permute-done | bytes 262176 | tf_op jit(solution)/shard_map/ppermute | solution.py:28
  45.0 0.0 collective-permute-start.5
  45.0 6.7 %collective-permute-done.5 = bf16[32,4096]{1,0:T(8,128)(2,1)S(1)} collective-permute-done((bf16[32,4096]{1,0:T(8,128)(2,1)S(1)}, bf16[32,4096]{1,0:T(8,128)(2,1)S(1)}, u32[]{:S(2)}, u32[]{:S(2)}) %collective-permute-start.5) | collective-permute-done | bytes 262176 | tf_op jit(solution)/shard_map/ppermute | solution.py:28
  51.7 0.0 collective-permute-start.6
  51.7 6.7 %collective-permute-done.6 = bf16[32,4096]{1,0:T(8,128)(2,1)S(1)} collective-permute-done((bf16[32,4096]{1,0:T(8,128)(2,1)S(1)}, bf16[32,4096]{1,0:T(8,128)(2,1)S(1)}, u32[]{:S(2)}, u32[]{:S(2)}) %collective-permute-start.6) | collective-permute-done | bytes 262176 | tf_op jit(solution)/shard_map/ppermute | solution.py:28
  58.4 0.4 fusion
  58.9 0.0 copy-start.1
  58.9 0.0 copy-start.3
  58.9 3.1 %fusion.3 = (f32[256]{0:T(256)S(1)}, f32[256,4096]{1,0:T(8,128)}) fusion(f32[4096]{0:T(1024)S(1)} %add_sqrt_fusion.1, bf16[256,4096]{1,0:T(8,128)(2,1)S(1)} %constant_dynamic-update-slice_fusion, bf16[256,256]{1,0:T(8,128)(2,1)S(1)} %copy-done.2, f32[256]{0:T(256)S(1)} %add_rsqrt_fusion.1), kind=kOutput, calls=%fused_computation.12 | convolution fusion | flops 540212992 | bytes 6440960 | tf_op jit(solution)/shard_map/dot_general | solution.py:37
  62.0 0.0 all-gather.2.cloned.1.call-done
  62.0 2.0 %multiply_reduce_fusion.1 = f32[4096]{0:T(1024)S(1)} fusion(bf16[256,4096]{1,0:T(8,128)(2,1)} %all-gather.2.cloned.1.call-done), kind=kLoop, calls=%fused_computation.10 | loop fusion | flops 3141632 | bytes 2113536 | tf_op jit(solution)/shard_map/reduce_sum | solution.py:33
  64.0 0.0 copy-done.1
  64.0 0.0 copy-done.3
  64.0 4.9 %fusion.16 = (f32[4096]{0:T(1024)S(1)}, f32[256]{0:T(256)S(1)}, f32[256,4096]{1,0:T(8,128)}) fusion(f32[4096]{0:T(1024)S(1)} %copy-done.3, f32[4096]{0:T(1024)S(1)} %add_sqrt_fusion, bf16[256,4096]{1,0:T(8,128)(2,1)} %all-gather.2.cloned.1.call-done, bf16[256,256]{1,0:T(8,128)(2,1)S(1)} %copy-done.1, f32[256]{0:T(256)S(1)} %add_rsqrt_fusion), kind=kOutput, calls=%fused_computation.39 | convolution fusion | flops 542306048 | bytes 6473728 | tf_op jit(solution)/shard_map/dot_general | solution.py:32
  69.0 11.7 %all-reduce = (f32[256]{0:T(256)S(1)}, f32[256]{0:T(256)S(1)}) all-reduce(f32[256]{0:T(256)S(1)} %get-tuple-element.4, f32[256]{0:T(256)S(1)} %get-tuple-element.12), channel_id=1, replica_groups=mesh['dp'=8,'tensor'=4] {'tensor'}, use_global_device_ids=true, to_apply=%region_7.8 | all-reduce | flops 512 | bytes 4096 | tf_op jit(solution)/shard_map/psum | solution.py:40
  80.6 4.5 %multiply_reduce_fusion = (f32[4096]{0:T(1024)S(1)}, bf16[256,4096]{1,0:T(8,128)(2,1)S(1)}) fusion(f32[256,4096]{1,0:T(8,128)} %get-tuple-element.13, f32[256]{0:T(256)S(1)} %get-tuple-element.5, f32[256,4096]{1,0:T(8,128)} %get-tuple-element.11, f32[4096]{0:T(1024)S(1)} %copy-done.3, f32[256]{0:T(256)S(1)} %get-tuple-element.6), kind=kLoop, calls=%fused_computation.7 | loop fusion | flops 11530240 | bytes 10520576 | tf_op jit(solution)/shard_map/reduce_sum | solution.py:46
  85.1 3.0 %fusion.2 = f32[256,4096]{1,0:T(8,128)} fusion(bf16[256,4096]{1,0:T(8,128)(2,1)S(1)} %constant_dynamic-update-slice_fusion, f32[4096]{0:T(1024)S(1)} %rsqrt_multiply_fusion, f32[4096]{0:T(1024)S(1)} %add_sqrt_fusion.1, bf16[256,4096]{1,0:T(8,128)(2,1)S(1)} %get-tuple-element.8, bf16[256,256]{1,0:T(8,128)(2,1)S(1)} %copy-done.2, f32[256]{0:T(256)S(1)} %add_rsqrt_fusion.1), kind=kOutput, calls=%fused_computation.6 | convolution fusion | flops 541261824 | bytes 8553472 | tf_op jit(solution)/shard_map/dot_general | solution.py:49
  88.1 0.0 reduce-scatter.2.cloned.1.call-update
  88.1 22.3 %psum.23 = f32[4096]{0:T(1024)S(1)} all-reduce(f32[4096]{0:T(1024)S(1)} %get-tuple-element.3), channel_id=1, replica_groups=mesh['dp'=8,'tensor'=4] {'dp'}, use_global_device_ids=true, to_apply=%region_11.12 | all-reduce | flops 4096 | bytes 32768 | tf_op jit(solution)/shard_map/psum | solution.py:43
  110.4 0.6 multiply_add_fusion.1
  111.0 26.3 %reduce-scatter.2.cloned.1.call-done = f32[32,4096]{1,0:T(8,128)} async-done(((f32[256,4096]{1,0:T(8,128)}), f32[32,4096]{1,0:T(8,128)}) %reduce-scatter.2.cloned.1.call-update) | async-done | bytes 524304 | tf_op jit(solution)/shard_map/reduce_scatter | solution.py:52
  (13 shorter events, 0.2 us)
Async XLA Ops:
  7.2 4.0 %copy-start = (bf16[32,4096]{1,0:T(8,128)(2,1)S(1)}, bf16[32,4096]{1,0:T(8,128)(2,1)}, u32[]{:S(2)}) copy-start(bf16[32,4096]{1,0:T(8,128)(2,1)} %param.6) | copy-start | bytes 786436
  7.2 4.1 %copy-start.2 = (bf16[256,256]{1,0:T(8,128)(2,1)S(1)}, bf16[256,256]{1,0:T(8,128)(2,1)}, u32[]{:S(2)}) copy-start(bf16[256,256]{1,0:T(8,128)(2,1)} %param.8) | copy-start | bytes 393220
  7.2 54.8 %all-gather.2.cloned.1.call-start = ((), (), s32[]{:S(2)}) async-start(), calls=%async_computation.1 | async-start | bytes 2359296 | tf_op jit(solution)/shard_map/all_gather | solution.py:30
  7.2 7.7 %collective-permute-start = (bf16[32,4096]{1,0:T(8,128)(2,1)}, bf16[32,4096]{1,0:T(8,128)(2,1)S(1)}, u32[]{:S(2)}, u32[]{:S(2)}) collective-permute-start(bf16[32,4096]{1,0:T(8,128)(2,1)} %param.6), channel_id=1, source_target_pairs={{0,4},{4,8},{8,12},{12,16},{16,20},{20,24},{24,28},{28,0},{1,5},{5... | collective-permute-start | bytes 786440 | tf_op jit(solution)/shard_map/ppermute | solution.py:28
  9.8 127.5 %reduce-scatter.2.cloned.1.call-start = ((), (), s32[]{:S(2)}) async-start(), calls=%async_computation.2 | async-start | bytes 4718592 | tf_op jit(solution)/shard_map/reduce_scatter | solution.py:52
  14.9 6.7 %collective-permute-start.1 = (bf16[32,4096]{1,0:T(8,128)(2,1)S(1)}, bf16[32,4096]{1,0:T(8,128)(2,1)S(1)}, u32[]{:S(2)}, u32[]{:S(2)}) collective-permute-start(bf16[32,4096]{1,0:T(8,128)(2,1)S(1)} %collective-permute-done), channel_id=1, source_target_pairs={{0,4},{4,8},{8,12},{12,16},{16,20},{20,24},{24,28},{28,0},{1,5},{5... | collective-permute-start | bytes 786440 | tf_op jit(solution)/shard_map/ppermute | solution.py:28
  21.6 8.2 %collective-permute-start.2 = (bf16[32,4096]{1,0:T(8,128)(2,1)S(1)}, bf16[32,4096]{1,0:T(8,128)(2,1)S(1)}, u32[]{:S(2)}, u32[]{:S(2)}) collective-permute-start(bf16[32,4096]{1,0:T(8,128)(2,1)S(1)} %collective-permute-done.1), channel_id=1, source_target_pairs={{0,4},{4,8},{8,12},{12,16},{16,20},{20,24},{24,28},{28,0},{1,5},{5... | collective-permute-start | bytes 786440 | tf_op jit(solution)/shard_map/ppermute | solution.py:28
  29.8 8.5 %collective-permute-start.3 = (bf16[32,4096]{1,0:T(8,128)(2,1)S(1)}, bf16[32,4096]{1,0:T(8,128)(2,1)S(1)}, u32[]{:S(2)}, u32[]{:S(2)}) collective-permute-start(bf16[32,4096]{1,0:T(8,128)(2,1)S(1)} %collective-permute-done.2), channel_id=1, source_target_pairs={{0,4},{4,8},{8,12},{12,16},{16,20},{20,24},{24,28},{28,0},{1,5},{5... | collective-permute-start | bytes 786440 | tf_op jit(solution)/shard_map/ppermute | solution.py:28
  38.3 6.7 %collective-permute-start.4 = (bf16[32,4096]{1,0:T(8,128)(2,1)S(1)}, bf16[32,4096]{1,0:T(8,128)(2,1)S(1)}, u32[]{:S(2)}, u32[]{:S(2)}) collective-permute-start(bf16[32,4096]{1,0:T(8,128)(2,1)S(1)} %collective-permute-done.3), channel_id=1, source_target_pairs={{0,4},{4,8},{8,12},{12,16},{16,20},{20,24},{24,28},{28,0},{1,5},{5... | collective-permute-start | bytes 786440 | tf_op jit(solution)/shard_map/ppermute | solution.py:28
  45.0 6.7 %collective-permute-start.5 = (bf16[32,4096]{1,0:T(8,128)(2,1)S(1)}, bf16[32,4096]{1,0:T(8,128)(2,1)S(1)}, u32[]{:S(2)}, u32[]{:S(2)}) collective-permute-start(bf16[32,4096]{1,0:T(8,128)(2,1)S(1)} %collective-permute-done.4), channel_id=1, source_target_pairs={{0,4},{4,8},{8,12},{12,16},{16,20},{20,24},{24,28},{28,0},{1,5},{5... | collective-permute-start | bytes 786440 | tf_op jit(solution)/shard_map/ppermute | solution.py:28
  51.7 6.7 %collective-permute-start.6 = (bf16[32,4096]{1,0:T(8,128)(2,1)S(1)}, bf16[32,4096]{1,0:T(8,128)(2,1)S(1)}, u32[]{:S(2)}, u32[]{:S(2)}) collective-permute-start(bf16[32,4096]{1,0:T(8,128)(2,1)S(1)} %collective-permute-done.5), channel_id=1, source_target_pairs={{0,4},{4,8},{8,12},{12,16},{16,20},{20,24},{24,28},{28,0},{1,5},{5... | collective-permute-start | bytes 786440 | tf_op jit(solution)/shard_map/ppermute | solution.py:28
  58.9 5.1 %copy-start.1 = (bf16[256,256]{1,0:T(8,128)(2,1)S(1)}, bf16[256,256]{1,0:T(8,128)(2,1)}, u32[]{:S(2)}) copy-start(bf16[256,256]{1,0:T(8,128)(2,1)} %param.7) | copy-start | bytes 393220
  58.9 5.1 %copy-start.3 = (f32[4096]{0:T(1024)S(1)}, f32[4096]{0:T(1024)}, u32[]{:S(2)}) copy-start(f32[4096]{0:T(1024)} %param.9) | copy-start | bytes 49156
Sparse Core Ops, SparseCore 0:
  10.5 33.2 all-gather.1
  88.2 49.0 reduce-scatter.1
